TPU v7x, 32 devices: a whole 2x2x4 slice. The times are simulated.
32 devices in a mesh: region: 8 (over y, x, core), dom: 4 (over z).
Axes of the slice: x: 2, y: 2, z: 4, core: 2. Of those that a mesh axis runs over, the one named last changes fastest.
Arguments:
- feats: bfloat16 [16384, 512], P(('region', 'dom')), may hold values from -6 to 6
- hub_feats: bfloat16 [64, 512], P('region'), may hold values from -6 to 6
- hub_ids: int32 [16384, 4], P(('region', 'dom')), may hold values from 0 to 63
- tile_src: int32 [512], P(('region', 'dom')), may hold values from 0 to 4
- tile_mask: int32 [512, 128, 128], P(('region', 'dom')), may hold values 0 or 1
- w_stack: bfloat16 [1024, 512], replicated, may hold values from -0.1875 to 0.1875
- cotangent: bfloat16 [16384, 512], P(('region', 'dom')), may hold values from -6 to 6
Outputs:
- activ: bfloat16 [16384, 512], P(('region', 'dom'))
- weight_grad: float32 [1024, 512], P('dom')
- hub_grad: float32 [64, 512], P('region')
Inputs may be any that keep to these rules, and one draw needn't show every extreme that they name: tile_src names a block of the part's window: 0 is the block taken from the previous part, 1 to 4 are the part's own blocks. `hub_ids`: hub ids index rows of hub_feats.
All inputs are finite; a program needn't handle non-finite values. No bound on the sum of `tile_mask` on one device may be relied on, other than what follows from the above.
Results may differ from a plain program's by a relative error of at most 0.0051.
Values may be sent and summed in bfloat16 or wider, within the bound.
No kernel may reach another device: no remote copies, remote signals or barrier semaphores. Data moves between devices by JAX's collectives and lax.ppermute only.
A program may use at most 64 MiB of HBM per device.

v0:
```python
import jax
import jax.numpy as jnp
from jax import lax
from jax.sharding import PartitionSpec as P


def shifted(value, axis, steps):
    count = lax.axis_size(axis)
    initial, last = (max(0, -steps), min(count, count - steps))
    return lax.ppermute(value, axis, [(source, source + steps) for source in range(initial, last)])


def on_device(feats, hub_feats, hub_ids, tile_src, tile_mask, w_stack, cotangent):
    rows, width = feats.shape
    tile = tile_mask.shape[1]
    nblk = rows // tile
    per_block = tile_src.shape[0] // nblk
    hub_count = hub_ids.shape[1]
    owned = hub_feats.shape[0]
    total_hubs = owned * lax.axis_size("region")
    prev = shifted(feats[rows - tile :], "dom", 1)
    window = jnp.concatenate([prev, feats], axis=0).reshape(nblk + 1, tile, width)
    picked = jnp.take(window, tile_src, axis=0)
    mask_b = tile_mask.astype(jnp.bfloat16)
    prod = jnp.einsum("tij,tjd->tid", mask_b, picked, preferred_element_type=jnp.float32)
    nsum = prod.reshape(nblk, per_block, tile, width).sum(axis=1).reshape(rows, width)
    cnt = tile_mask.reshape(nblk, per_block, tile, tile).sum(axis=(1, 3)).reshape(rows)
    deg = 1.0 + cnt.astype(jnp.float32) + jnp.float32(hub_count)
    hub_cols = lax.broadcasted_iota(jnp.int32, (rows, total_hubs), 1)
    counts = jnp.zeros((rows, total_hubs), jnp.float32)
    for slot in range(hub_count):
        counts = counts + (hub_ids[:, slot : slot + 1] == hub_cols).astype(jnp.float32)
    counts = counts.astype(jnp.bfloat16)
    block = counts
    hsum = jnp.dot(
        block,
        lax.all_gather(hub_feats, "region", axis=0, tiled=True),
        preferred_element_type=jnp.float32,
    )
    agg = ((feats.astype(jnp.float32) + nsum + hsum) / deg[:, None]).astype(jnp.bfloat16)
    inputs = jnp.concatenate([feats, agg], axis=1)
    z = jnp.dot(inputs, w_stack, preferred_element_type=jnp.float32)
    sig = jax.nn.sigmoid(z)
    activ = (z * sig).astype(jnp.bfloat16)
    dz = (cotangent.astype(jnp.float32) * sig * (1.0 + z * (1.0 - sig))).astype(jnp.bfloat16)
    partial_w = lax.psum_scatter(
        lax.dot_general(inputs, dz, (((0,), (0,)), ((), ())), preferred_element_type=jnp.float32),
        "dom",
        scatter_dimension=0,
        tiled=True,
    )
    weight_grad = lax.psum(partial_w, "region")
    dagg = lax.dot_general(
        dz, w_stack[width:], (((1,), (1,)), ((), ())), preferred_element_type=jnp.float32
    )
    sgrad = (dagg / deg[:, None]).astype(jnp.bfloat16)
    block = counts
    region_sum = lax.psum_scatter(
        lax.dot_general(block, sgrad, (((0,), (0,)), ((), ())), preferred_element_type=jnp.float32),
        "region",
        scatter_dimension=0,
        tiled=True,
    )
    hub_grad = lax.psum(region_sum, "dom")
    return (activ, weight_grad, hub_grad)


def solution(mesh):
    placed = (
        P(("region", "dom"), None),
        P("region", None),
        P(("region", "dom"), None),
        P(("region", "dom")),
        P(("region", "dom"), None, None),
        P(),
        P(("region", "dom"), None),
    )
    return jax.shard_map(
        on_device,
        mesh=mesh,
        in_specs=placed,
        out_specs=(P(("region", "dom"), None), P("dom", None), P("region", None)),
        check_vma=False,
    )
```

profile of v0, /device:TPU:0, one launch (start us, length us, event | category | flops | bytes accessed | tf_op | source)
XLA Modules:
  0.0 183.3 jit_solution(3585333480241991576)
XLA Ops:
  7.2 0.0 reduce-scatter.3.cloned.1.call-start
  7.2 1.0 slice.18
  8.2 5.0 %collective-permute-start = (bf16[128,512]{1,0:T(8,128)(2,1)S(1)}, bf16[128,512]{1,0:T(8,128)(2,1)S(1)}, u32[]{:S(2)}, u32[]{:S(2)}) collective-permute-start(bf16[128,512]{1,0:T(8,128)(2,1)S(1)} %slice.18), channel_id=1, source_target_pairs={{0,1},{1,2},{2,3},{4,5},{5,6},{6,7},{8,9},{9,10},{10,11},{12,13},{... | collective-permute-start | bytes 393224 | tf_op jit(solution)/shard_map/ppermute | solution.py:10
  13.2 1.6 reduce_sum.26
  14.8 0.9 fusion.19
  15.6 0.7 compare_select_fusion
  16.3 0.7 compare_and_fusion
  17.0 1.3 copy.23
  18.2 9.3 %all_gather.3 = bf16[64,512]{1,0:T(8,128)(2,1)S(1)} all-gather(bf16[8,512]{1,0:T(8,128)(2,1)S(1)} %copy-done.2), channel_id=1, replica_groups=mesh['region'=8,'dom'=4] {'region'}, dimensions={0}, use_global_device_ids=true | all-gather | bytes 73728 | tf_op jit(solution)/shard_map/all_gather | solution.py:37
  27.6 2.0 %gather_fusion = bf16[16,128,512]{2,1,0:T(8,128)(2,1)} fusion(bf16[5,128,512]{2,1,0:T(8,128)(2,1)S(1)} %bitcast.23, s32[1024]{0:T(1024)S(1)} %pad_clamp_fusion), kind=kCustom, calls=%fused_computation | custom fusion | bytes 4194368 | tf_op jit(solution)/shard_map/jit(_take)/gather | solution.py:23
  29.6 2.6 %bitcast_reduce_fusion = f32[4,128,512]{1,2,0:T(8,128)S(1)} fusion(bf16[16,128,512]{2,1,0:T(8,128)(2,1)} %gather_fusion, pred[16]{0:T(512)(128)(4,1)S(1)} %compare_and_fusion, s32[16,128,128]{2,1,0:T(8,128)S(1)} %copy-done.1), kind=kOutput, calls=%fused_computation.1 | convolution fusion | flops 270532608 | bytes 4194320 | tf_op jit(solution)/shard_map/tij,tjd->tid/dot_general | solution.py:25
  32.2 1.0 fusion.6
  33.2 0.2 copy-done.3
  33.4 0.1 copy-done.4
  33.6 1.9 %multiply_convert_fusion = (bf16[512,512]{1,0:T(8,128)(2,1)S(1)}, bf16[512,512]{1,0:T(8,128)(2,1)}) fusion(bf16[512,512]{1,0:T(8,128)(2,1)S(1)} %copy-done.4, bf16[1024,512]{1,0:T(8,128)(2,1)S(1)} %copy-done.3, bf16[512,512]{0,1:T(8,128)(2,1)S(1)} %fusion.6, bf16[512,512]{0,1:T(8,128)(2,1)S(1)} %copy.23), kind=kOutput, calls=%fused_computation.13 | convolution fusion | flops 542113792 | bytes 3670016 | tf_op jit(solution)/shard_map/dot_general | solution.py:42
  35.5 2.1 %fusion.10 = f32[1024,512]{1,0:T(8,128)} fusion(bf16[512,512]{1,0:T(8,128)(2,1)S(1)} %get-tuple-element.3, bf16[512,512]{0,1:T(8,128)(2,1)S(1)} %fusion.6, bf16[512,512]{0,1:T(8,128)(2,1)S(1)} %copy.23), kind=kOutput, calls=%fused_computation.17 | convolution fusion | flops 538968064 | bytes 3670016 | tf_op jit(solution)/shard_map/dot_general | solution.py:47
  37.6 0.0 reduce-scatter.5.cloned.1.call-start
  37.6 1.3 fusion.8
  39.0 0.0 all-reduce.2.cloned.1.call-start
  39.0 41.6 %reduce-scatter.3.cloned.1.call-done = f32[256,512]{1,0:T(8,128)} async-done(((f32[1024,512]{1,0:T(8,128)}), f32[256,512]{1,0:T(8,128)}) %reduce-scatter.3.cloned.1.call-update) | async-done | bytes 524304 | tf_op jit(solution)/shard_map/reduce_scatter | solution.py:46
  80.7 36.3 %reduce-scatter.5.cloned.1.call-done = f32[8,512]{1,0:T(8,128)} async-done(((f32[64,512]{1,0:T(8,128)}), f32[8,512]{1,0:T(8,128)}) %reduce-scatter.5.cloned.1.call-update) | async-done | bytes 16400 | tf_op jit(solution)/shard_map/reduce_scatter | solution.py:58
  117.0 19.9 %psum.15 = f32[8,512]{1,0:T(8,128)} all-reduce(f32[8,512]{1,0:T(8,128)} %reduce-scatter.5.cloned.1.call-done), channel_id=1, replica_groups=mesh['region'=8,'dom'=4] {'dom'}, use_global_device_ids=true, to_apply=%region_6.7 | all-reduce | flops 4096 | bytes 32768 | tf_op jit(solution)/shard_map/psum | solution.py:64
  136.9 38.0 %all-reduce.2.cloned.1.call-done = f32[256,512]{1,0:T(8,128)} async-done(((f32[256,512]{1,0:T(8,128)}), f32[256,512]{1,0:T(8,128)}) %all-reduce.2.cloned.1.call-update) | async-done | bytes 524304 | tf_op jit(solution)/shard_map/psum | solution.py:52
  174.9 1.9 %copy.30 = f32[256,512]{1,0:T(8,128)} copy(f32[256,512]{1,0:T(8,128)} %all-reduce.2.cloned.1.call-done) | data formatting | bytes 1048576
  (16 shorter events, 0.2 us)
Async XLA Ops:
  7.2 20.3 %copy-start = (bf16[512,512]{1,0:T(8,128)(2,1)S(1)}, bf16[512,512]{1,0:T(8,128)(2,1)}, u32[]{:S(2)}) copy-start(bf16[512,512]{1,0:T(8,128)(2,1)} %param.7) | copy-start | bytes 1572868
  7.2 11.0 %copy-start.2 = (bf16[8,512]{1,0:T(8,128)(2,1)S(1)}, bf16[8,512]{1,0:T(8,128)(2,1)}, u32[]{:S(2)}) copy-start(bf16[8,512]{1,0:T(8,128)(2,1)} %param.8) | copy-start | bytes 24580
  7.2 73.4 %reduce-scatter.3.cloned.1.call-start = ((), (), s32[]{:S(2)}) async-start(), calls=%async_computation.2 | async-start | bytes 2621440 | tf_op jit(solution)/shard_map/reduce_scatter | solution.py:46
  8.2 19.3 %collective-permute-start = (bf16[128,512]{1,0:T(8,128)(2,1)S(1)}, bf16[128,512]{1,0:T(8,128)(2,1)S(1)}, u32[]{:S(2)}, u32[]{:S(2)}) collective-permute-start(bf16[128,512]{1,0:T(8,128)(2,1)S(1)} %slice.18), channel_id=1, source_target_pairs={{0,1},{1,2},{2,3},{4,5},{5,6},{6,7},{8,9},{9,10},{10,11},{12,13},{... | collective-permute-start | bytes 393224 | tf_op jit(solution)/shard_map/ppermute | solution.py:10
  27.6 2.0 %copy-start.1 = (s32[16,128,128]{2,1,0:T(8,128)S(1)}, s32[16,128,128]{2,1,0:T(8,128)}, u32[]{:S(2)}) copy-start(s32[16,128,128]{2,1,0:T(8,128)} %param.11) | copy-start | bytes 3145732
  32.2 1.2 copy-start.3
  32.2 1.3 copy-start.4
  37.6 79.4 %reduce-scatter.5.cloned.1.call-start = ((), (), s32[]{:S(2)}) async-start(), calls=%async_computation.4 | async-start | bytes 147456 | tf_op jit(solution)/shard_map/reduce_scatter | solution.py:58
  39.0 135.9 %all-reduce.2.cloned.1.call-start = ((), (), s32[]{:S(2)}) async-start(), calls=%async_computation.3 | async-start | bytes 1048576 | tf_op jit(solution)/shard_map/psum | solution.py:52
Sparse Core Ops, SparseCore 0:
  37.7 42.8 reduce-scatter.2
  84.2 32.7 reduce-scatter.4
  120.1 54.7 all-reduce.1
where the time goes:
time: 184 us; the launch traced here: 183 us
  waiting for transfers between devices  116 us (63%)
  blocking collectives  29.2 us (16%)
  between operations  13.9 us (8%)
  matrix products  8.9 us (5%)
  local copies, waits for them, and re-layouts  7.35 us (4%)
  starting transfers between devices  5.08 us (3%)
  other arithmetic  2.97 us (2%)
    reduce_scatter x1, waiting for transfers between devices, on_device(): lax.psum_scatter(lax.dot_general(inputs, dz, (((0,), (0,)), ((), ())), pr...  41.6 us
    psum x1, waiting for transfers between devices, on_device(): weight_grad = lax.psum(partial_w, 'region')  38 us
    reduce_scatter x1, waiting for transfers between devices, on_device(): lax.psum_scatter(lax.dot_general(block, sgrad, (((0,), (0,)), ((), ())),...  36.3 us
    psum x1, blocking collectives, on_device(): hub_grad = lax.psum(region_sum, 'dom')  19.9 us
    all_gather x1, blocking collectives, on_device(): lax.all_gather(hub_feats, 'region', axis=0, tiled=True)  9.26 us
    ppermute x1, starting transfers between devices, shifted(): lax.ppermute(value, axis, [(source, source + steps) for source in range(i...  4.96 us
  transfers between devices with their start and end apart: 4, of which 3 were waited for; matrix products, arithmetic and copies ran while one was open for 3% of the time, Pallas kernels for 0%

commit v1 on v0

--- a/solution.py
+++ b/solution.py
@@ -2,6 +2,24 @@
 import jax.numpy as jnp
 from jax import lax
 from jax.sharding import PartitionSpec as P
+
+
+def ring_gather(array, axis, dim):
+    ways, here, step = (lax.axis_size(axis), lax.axis_index(axis), array.shape[dim])
+    shape = [n * ways if d == dim else n for d, n in enumerate(array.shape)]
+    full = lax.dynamic_update_slice_in_dim(
+        jnp.zeros(shape, array.dtype), array, here * step, axis=dim
+    )
+    going_up = going_down = array
+    for far in range(1, ways // 2 + 1):
+        going_up = lax.ppermute(going_up, axis, [(d, (d + 1) % ways) for d in range(ways)])
+        full = lax.dynamic_update_slice_in_dim(full, going_up, (here - far) % ways * step, axis=dim)
+        if 2 * far < ways:
+            going_down = lax.ppermute(going_down, axis, [(d, (d - 1) % ways) for d in range(ways)])
+            full = lax.dynamic_update_slice_in_dim(
+                full, going_down, (here + far) % ways * step, axis=dim
+            )
+    return full
 
 
 def shifted(value, axis, steps):
@@ -32,11 +50,7 @@
         counts = counts + (hub_ids[:, slot : slot + 1] == hub_cols).astype(jnp.float32)
     counts = counts.astype(jnp.bfloat16)
     block = counts
-    hsum = jnp.dot(
-        block,
-        lax.all_gather(hub_feats, "region", axis=0, tiled=True),
-        preferred_element_type=jnp.float32,
-    )
+    hsum = jnp.dot(block, ring_gather(hub_feats, "region", 0), preferred_element_type=jnp.float32)
     agg = ((feats.astype(jnp.float32) + nsum + hsum) / deg[:, None]).astype(jnp.bfloat16)
     inputs = jnp.concatenate([feats, agg], axis=1)
     z = jnp.dot(inputs, w_stack, preferred_element_type=jnp.float32)

time: 184 us -> 190 us (1.033)
  blocking collectives: 29.2 us -> 20 us
  starting transfers between devices: 5.08 us -> 13.1 us
  waiting for transfers between devices: 116 us -> 123 us
    all_gather x1 -> x0, blocking collectives: 9.26 us -> none  [on_device(): lax.all_gather(hub_feats, 'region', axis=0, tiled=True)]
    ppermute x0 -> x7, starting transfers between devices: none -> 8.78 us  [the longest x3 8.17 us: ring_gather(): lax.ppermute(going_down, axis, [(d, (d - 1) % ways) for d in range(ways)])]
    ppermute x0 -> x7, waiting for transfers between devices: none -> 6.65 us  [the longest x4 6.58 us: ring_gather(): lax.ppermute(going_up, axis, [(d, (d + 1) % ways) for d in range(ways)])]
  transfers between devices with their start and end apart: 4 -> 11, of which waited for: 3 -> 6; matrix products, arithmetic and copies ran while one was open for 3% -> 4% of each run, Pallas kernels for 0% -> 0%
where the time goes in v1:
time: 190 us; the launch traced here: 189 us
  waiting for transfers between devices  123 us (65%)
  blocking collectives  20 us (11%)
  between operations  13.9 us (7%)
  starting transfers between devices  13.1 us (7%)
  matrix products  8.88 us (5%)
  local copies, waits for them, and re-layouts  8 us (4%)
  other arithmetic  2.96 us (2%)
    reduce_scatter x1, waiting for transfers between devices, on_device(): lax.psum_scatter(lax.dot_general(inputs, dz, (((0,), (0,)), ((), ())), pr...  41.6 us
    psum x1, waiting for transfers between devices, on_device(): weight_grad = lax.psum(partial_w, 'region')  38 us
    reduce_scatter x1, waiting for transfers between devices, on_device(): lax.psum_scatter(lax.dot_general(block, sgrad, (((0,), (0,)), ((), ())),...  36.3 us
    psum x1, blocking collectives, on_device(): hub_grad = lax.psum(region_sum, 'dom')  20 us
    ppermute x3, starting transfers between devices, ring_gather(): lax.ppermute(going_down, axis, [(d, (d - 1) % ways) for d in range(ways)])  8.17 us
    ppermute x4, waiting for transfers between devices, ring_gather(): lax.ppermute(going_up, axis, [(d, (d + 1) % ways) for d in range(ways)])  6.58 us
    ppermute x1, starting transfers between devices, shifted(): lax.ppermute(value, axis, [(source, source + steps) for source in range(i...  4.18 us
  transfers between devices with their start and end apart: 11, of which 6 were waited for; matrix products, arithmetic and copies ran while one was open for 4% of the time, Pallas kernels for 0%

profile of v1, /device:TPU:0, one launch (start us, length us, event | category | flops | bytes accessed | tf_op | source)
XLA Modules:
  0.0 189.5 jit_solution(17576235610270385420)
XLA Ops:
  7.8 2.9 %collective-permute-start.2 = (bf16[8,512]{1,0:T(8,128)(2,1)}, bf16[8,512]{1,0:T(8,128)(2,1)S(1)}, u32[]{:S(2)}, u32[]{:S(2)}) collective-permute-start(bf16[8,512]{1,0:T(8,128)(2,1)} %param.8), channel_id=1, source_target_pairs={{0,28},{4,0},{8,4},{12,8},{16,12},{20,16},{24,20},{28,24},{1,29},{... | collective-permute-start | bytes 24584 | tf_op jit(solution)/shard_map/ppermute | solution.py:18
  10.7 0.9 slice.18
  11.6 4.2 %collective-permute-start = (bf16[128,512]{1,0:T(8,128)(2,1)S(1)}, bf16[128,512]{1,0:T(8,128)(2,1)S(1)}, u32[]{:S(2)}, u32[]{:S(2)}) collective-permute-start(bf16[128,512]{1,0:T(8,128)(2,1)S(1)} %slice.18), channel_id=1, source_target_pairs={{0,1},{1,2},{2,3},{4,5},{5,6},{6,7},{8,9},{9,10},{10,11},{12,13},{... | collective-permute-start | bytes 393224 | tf_op jit(solution)/shard_map/ppermute | solution.py:28
  16.5 0.7 compare_and_fusion
  17.1 1.6 reduce_sum.26
  18.7 0.9 fusion.19
  19.6 0.7 constant_dynamic-update-slice_fusion.7
  20.3 1.3 copy.23
  21.7 2.6 %collective-permute-start.4 = (bf16[8,512]{1,0:T(8,128)(2,1)S(1)}, bf16[8,512]{1,0:T(8,128)(2,1)S(1)}, u32[]{:S(2)}, u32[]{:S(2)}) collective-permute-start(bf16[8,512]{1,0:T(8,128)(2,1)S(1)} %collective-permute-done.2), channel_id=1, source_target_pairs={{0,28},{4,0},{8,4},{12,8},{16,12},{20,16},{24,20},{28,24},{1,29},{... | collective-permute-start | bytes 24584 | tf_op jit(solution)/shard_map/ppermute | solution.py:18
  24.3 1.3 collective-permute-done.3
  25.7 2.6 %collective-permute-start.6 = (bf16[8,512]{1,0:T(8,128)(2,1)S(1)}, bf16[8,512]{1,0:T(8,128)(2,1)S(1)}, u32[]{:S(2)}, u32[]{:S(2)}) collective-permute-start(bf16[8,512]{1,0:T(8,128)(2,1)S(1)} %collective-permute-done.4), channel_id=1, source_target_pairs={{0,28},{4,0},{8,4},{12,8},{16,12},{20,16},{24,20},{28,24},{1,29},{... | collective-permute-start | bytes 24584 | tf_op jit(solution)/shard_map/ppermute | solution.py:18
  28.3 1.3 collective-permute-done.5
  29.7 3.9 %collective-permute-done.7 = bf16[8,512]{1,0:T(8,128)(2,1)S(1)} collective-permute-done((bf16[8,512]{1,0:T(8,128)(2,1)S(1)}, bf16[8,512]{1,0:T(8,128)(2,1)S(1)}, u32[]{:S(2)}, u32[]{:S(2)}) %collective-permute-start.7) | collective-permute-done | bytes 8224 | tf_op jit(solution)/shard_map/ppermute | solution.py:15
  33.7 2.0 %gather_fusion = bf16[16,128,512]{2,1,0:T(8,128)(2,1)} fusion(bf16[5,128,512]{2,1,0:T(8,128)(2,1)S(1)} %bitcast.23, s32[1024]{0:T(1024)S(1)} %pad_clamp_fusion), kind=kCustom, calls=%fused_computation | custom fusion | bytes 4194368 | tf_op jit(solution)/shard_map/jit(_take)/gather | solution.py:41
  35.7 2.6 %bitcast_reduce_fusion = f32[4,128,512]{1,2,0:T(8,128)S(1)} fusion(bf16[16,128,512]{2,1,0:T(8,128)(2,1)} %gather_fusion, pred[16]{0:T(512)(128)(4,1)S(1)} %compare_and_fusion, s32[16,128,128]{2,1,0:T(8,128)S(1)} %copy-done.1), kind=kOutput, calls=%fused_computation.1 | convolution fusion | flops 270532608 | bytes 4194320 | tf_op jit(solution)/shard_map/tij,tjd->tid/dot_general | solution.py:43
  38.3 1.0 fusion.6
  39.7 1.9 %multiply_convert_fusion = (bf16[512,512]{1,0:T(8,128)(2,1)S(1)}, bf16[512,512]{1,0:T(8,128)(2,1)}) fusion(bf16[512,512]{1,0:T(8,128)(2,1)S(1)} %copy-done.3, bf16[1024,512]{1,0:T(8,128)(2,1)S(1)} %copy-done.2, bf16[512,512]{0,1:T(8,128)(2,1)S(1)} %fusion.6, bf16[512,512]{0,1:T(8,128)(2,1)S(1)} %copy.23), kind=kOutput, calls=%fused_computation.13 | convolution fusion | flops 542113792 | bytes 3670016 | tf_op jit(solution)/shard_map/dot_general | solution.py:56
  41.6 2.0 %fusion.10 = f32[1024,512]{1,0:T(8,128)} fusion(bf16[512,512]{1,0:T(8,128)(2,1)S(1)} %get-tuple-element.3, bf16[512,512]{0,1:T(8,128)(2,1)S(1)} %fusion.6, bf16[512,512]{0,1:T(8,128)(2,1)S(1)} %copy.23), kind=kOutput, calls=%fused_computation.17 | convolution fusion | flops 538968064 | bytes 3670016 | tf_op jit(solution)/shard_map/dot_general | solution.py:61
  43.7 1.3 fusion.8
  45.1 41.6 %reduce-scatter.3.cloned.1.call-done = f32[256,512]{1,0:T(8,128)} async-done(((f32[1024,512]{1,0:T(8,128)}), f32[256,512]{1,0:T(8,128)}) %reduce-scatter.3.cloned.1.call-update) | async-done | bytes 524304 | tf_op jit(solution)/shard_map/reduce_scatter | solution.py:60
  86.8 36.3 %reduce-scatter.5.cloned.1.call-done = f32[8,512]{1,0:T(8,128)} async-done(((f32[64,512]{1,0:T(8,128)}), f32[8,512]{1,0:T(8,128)}) %reduce-scatter.5.cloned.1.call-update) | async-done | bytes 16400 | tf_op jit(solution)/shard_map/reduce_scatter | solution.py:72
  123.1 20.0 %psum.15 = f32[8,512]{1,0:T(8,128)} all-reduce(f32[8,512]{1,0:T(8,128)} %reduce-scatter.5.cloned.1.call-done), channel_id=1, replica_groups=mesh['region'=8,'dom'=4] {'dom'}, use_global_device_ids=true, to_apply=%region_6.7 | all-reduce | flops 4096 | bytes 32768 | tf_op jit(solution)/shard_map/psum | solution.py:78
  143.1 38.0 %all-reduce.2.cloned.1.call-done = f32[256,512]{1,0:T(8,128)} async-done(((f32[256,512]{1,0:T(8,128)}), f32[256,512]{1,0:T(8,128)}) %all-reduce.2.cloned.1.call-update) | async-done | bytes 524304 | tf_op jit(solution)/shard_map/psum | solution.py:66
  181.1 1.9 copy.38
  (36 shorter events, 2.0 us)
Async XLA Ops:
  7.2 26.5 %copy-start = (bf16[512,512]{1,0:T(8,128)(2,1)S(1)}, bf16[512,512]{1,0:T(8,128)(2,1)}, u32[]{:S(2)}) copy-start(bf16[512,512]{1,0:T(8,128)(2,1)} %param.7) | copy-start | bytes 1572868
  7.2 79.6 %reduce-scatter.3.cloned.1.call-start = ((), (), s32[]{:S(2)}) async-start(), calls=%async_computation.2 | async-start | bytes 2621440 | tf_op jit(solution)/shard_map/reduce_scatter | solution.py:60
  7.2 14.4 %collective-permute-start.1 = (bf16[8,512]{1,0:T(8,128)(2,1)}, bf16[8,512]{1,0:T(8,128)(2,1)S(1)}, u32[]{:S(2)}, u32[]{:S(2)}) collective-permute-start(bf16[8,512]{1,0:T(8,128)(2,1)} %param.8), channel_id=1, source_target_pairs={{0,4},{4,8},{8,12},{12,16},{16,20},{20,24},{24,28},{28,0},{1,5},{5... | collective-permute-start | bytes 24584 | tf_op jit(solution)/shard_map/ppermute | solution.py:15
  7.8 13.9 %collective-permute-start.2 = (bf16[8,512]{1,0:T(8,128)(2,1)}, bf16[8,512]{1,0:T(8,128)(2,1)S(1)}, u32[]{:S(2)}, u32[]{:S(2)}) collective-permute-start(bf16[8,512]{1,0:T(8,128)(2,1)} %param.8), channel_id=1, source_target_pairs={{0,28},{4,0},{8,4},{12,8},{16,12},{20,16},{24,20},{28,24},{1,29},{... | collective-permute-start | bytes 24584 | tf_op jit(solution)/shard_map/ppermute | solution.py:18
  11.6 22.0 %collective-permute-start = (bf16[128,512]{1,0:T(8,128)(2,1)S(1)}, bf16[128,512]{1,0:T(8,128)(2,1)S(1)}, u32[]{:S(2)}, u32[]{:S(2)}) collective-permute-start(bf16[128,512]{1,0:T(8,128)(2,1)S(1)} %slice.18), channel_id=1, source_target_pairs={{0,1},{1,2},{2,3},{4,5},{5,6},{6,7},{8,9},{9,10},{10,11},{12,13},{... | collective-permute-start | bytes 393224 | tf_op jit(solution)/shard_map/ppermute | solution.py:28
  21.6 4.0 %collective-permute-start.3 = (bf16[8,512]{1,0:T(8,128)(2,1)S(1)}, bf16[8,512]{1,0:T(8,128)(2,1)S(1)}, u32[]{:S(2)}, u32[]{:S(2)}) collective-permute-start(bf16[8,512]{1,0:T(8,128)(2,1)S(1)} %collective-permute-done.1), channel_id=1, source_target_pairs={{0,4},{4,8},{8,12},{12,16},{16,20},{20,24},{24,28},{28,0},{1,5},{5... | collective-permute-start | bytes 24584 | tf_op jit(solution)/shard_map/ppermute | solution.py:15
  21.7 4.0 %collective-permute-start.4 = (bf16[8,512]{1,0:T(8,128)(2,1)S(1)}, bf16[8,512]{1,0:T(8,128)(2,1)S(1)}, u32[]{:S(2)}, u32[]{:S(2)}) collective-permute-start(bf16[8,512]{1,0:T(8,128)(2,1)S(1)} %collective-permute-done.2), channel_id=1, source_target_pairs={{0,28},{4,0},{8,4},{12,8},{16,12},{20,16},{24,20},{28,24},{1,29},{... | collective-permute-start | bytes 24584 | tf_op jit(solution)/shard_map/ppermute | solution.py:18
  25.7 4.0 %collective-permute-start.5 = (bf16[8,512]{1,0:T(8,128)(2,1)S(1)}, bf16[8,512]{1,0:T(8,128)(2,1)S(1)}, u32[]{:S(2)}, u32[]{:S(2)}) collective-permute-start(bf16[8,512]{1,0:T(8,128)(2,1)S(1)} %collective-permute-done.3), channel_id=1, source_target_pairs={{0,4},{4,8},{8,12},{12,16},{16,20},{20,24},{24,28},{28,0},{1,5},{5... | collective-permute-start | bytes 24584 | tf_op jit(solution)/shard_map/ppermute | solution.py:15
  25.7 4.0 %collective-permute-start.6 = (bf16[8,512]{1,0:T(8,128)(2,1)S(1)}, bf16[8,512]{1,0:T(8,128)(2,1)S(1)}, u32[]{:S(2)}, u32[]{:S(2)}) collective-permute-start(bf16[8,512]{1,0:T(8,128)(2,1)S(1)} %collective-permute-done.4), channel_id=1, source_target_pairs={{0,28},{4,0},{8,4},{12,8},{16,12},{20,16},{24,20},{28,24},{1,29},{... | collective-permute-start | bytes 24584 | tf_op jit(solution)/shard_map/ppermute | solution.py:18
  29.6 4.0 %collective-permute-start.7 = (bf16[8,512]{1,0:T(8,128)(2,1)S(1)}, bf16[8,512]{1,0:T(8,128)(2,1)S(1)}, u32[]{:S(2)}, u32[]{:S(2)}) collective-permute-start(bf16[8,512]{1,0:T(8,128)(2,1)S(1)} %collective-permute-done.5), channel_id=1, source_target_pairs={{0,4},{4,8},{8,12},{12,16},{16,20},{20,24},{24,28},{28,0},{1,5},{5... | collective-permute-start | bytes 24584 | tf_op jit(solution)/shard_map/ppermute | solution.py:15
  33.7 2.0 %copy-start.1 = (s32[16,128,128]{2,1,0:T(8,128)S(1)}, s32[16,128,128]{2,1,0:T(8,128)}, u32[]{:S(2)}) copy-start(s32[16,128,128]{2,1,0:T(8,128)} %param.11) | copy-start | bytes 3145732
  38.3 1.2 copy-start.2
  38.3 1.3 copy-start.3
  43.7 79.5 %reduce-scatter.5.cloned.1.call-start = ((), (), s32[]{:S(2)}) async-start(), calls=%async_computation.4 | async-start | bytes 147456 | tf_op jit(solution)/shard_map/reduce_scatter | solution.py:72
  45.1 136.0 %all-reduce.2.cloned.1.call-start = ((), (), s32[]{:S(2)}) async-start(), calls=%async_computation.3 | async-start | bytes 1048576 | tf_op jit(solution)/shard_map/psum | solution.py:66
Sparse Core Ops, SparseCore 0:
  43.8 42.9 reduce-scatter.2
  90.3 32.7 reduce-scatter.4
  126.2 54.7 all-reduce.1
